TPU v7x, 512 devices: a whole 4x4x16 slice. The times are simulated.
512 devices in a mesh: rep: 4 (over z_hi), exp: 16 (over x, y), mdl: 8 (over z_lo, core).
Axes of the slice: x: 4, y: 4, z: 16 (z_hi: 4, z_lo: 4; z = z_hi * 4 + z_lo), core: 2. Of those that a mesh axis runs over, the one named last changes fastest.
Arguments:
- inner_experts: bfloat16 [4, 16, 2, 768, 2048], P('rep', 'exp', None, None, 'mdl'), may hold values from -6 to 6
- inner_dense: bfloat16 [4, 9216, 768], P('rep', ('exp', 'mdl')), may hold values from -6 to 6
- inner_small: bfloat16 [4, 18, 768], P('rep'), may hold values from -6 to 6
- inner_embed: bfloat16 [4, 8192, 768], P('rep', ('exp', 'mdl')), may hold values from -6 to 6
- outer_experts: float32 [16, 2, 768, 2048], P('exp', None, ('rep', 'mdl')), may hold values from -6 to 6
- outer_dense: float32 [9216, 768], P(('exp', 'mdl'), 'rep'), may hold values from -6 to 6
- outer_small: float32 [18, 768], P(None, 'rep'), may hold values from -6 to 6
- outer_embed: float32 [8192, 768], P(('exp', 'mdl'), 'rep'), may hold values from -6 to 6
- moment_experts: float32 [16, 2, 768, 2048], P('exp', None, ('rep', 'mdl')), may hold values from -3 to 3
- moment_dense: float32 [9216, 768], P(('exp', 'mdl'), 'rep'), may hold values from -3 to 3
- moment_small: float32 [18, 768], P(None, 'rep'), may hold values from -3 to 3
- moment_embed: float32 [8192, 768], P(('exp', 'mdl'), 'rep'), may hold values from -3 to 3
- embed_basis: float32 [768, 64], replicated, may hold values from -0.21875 to 0.21875
Outputs:
- new_outer_experts: float32 [16, 2, 768, 2048], P('exp', None, ('rep', 'mdl'))
- new_moment_experts: float32 [16, 2, 768, 2048], P('exp', None, ('rep', 'mdl'))
- copy_experts: bfloat16 [16, 2, 768, 2048], P('exp', None, None, 'mdl')
- new_outer_dense: float32 [9216, 768], P(('exp', 'mdl'), 'rep')
- new_moment_dense: float32 [9216, 768], P(('exp', 'mdl'), 'rep')
- copy_dense: bfloat16 [9216, 768], P(('exp', 'mdl'))
- new_outer_small: float32 [18, 768], P(None, 'rep')
- new_moment_small: float32 [18, 768], P(None, 'rep')
- copy_small: bfloat16 [18, 768], replicated
- new_outer_embed: float32 [8192, 768], P(('exp', 'mdl'), 'rep')
- new_moment_embed: float32 [8192, 768], P(('exp', 'mdl'), 'rep')
- copy_embed: bfloat16 [8192, 768], P(('exp', 'mdl'))
All inputs are finite; a program needn't handle non-finite values.
Results may differ from a plain program's by a relative error of at most 0.012.
Values may be sent and summed in bfloat16 or wider, within the bound.
No kernel may reach another device: no remote copies, remote signals or barrier semaphores. Data moves between devices by JAX's collectives and lax.ppermute only.
A program may use at most 64 MiB of HBM per device.

v0:
```python
import jax
import jax.numpy as jnp
from jax import lax
from jax.sharding import PartitionSpec as P

decay_rate = 0.5
outer_rate = 0.7


def nesterov(outer, moment, grad_value):
    moment_new = decay_rate * moment + grad_value
    outer_new = outer - outer_rate * (grad_value + decay_rate * moment_new)
    return (outer_new, moment_new)


def on_device(
    inner_experts,
    inner_dense,
    inner_small,
    inner_embed,
    outer_experts,
    outer_dense,
    outer_small,
    outer_embed,
    moment_experts,
    moment_dense,
    moment_small,
    moment_embed,
    embed_basis,
):
    groups = lax.axis_size("rep")
    own_shard = inner_experts[0, 0]
    row_count = outer_experts.shape[2]
    full_width = outer_experts.shape[3]
    pieces = lax.all_to_all(own_shard, ("rep", "mdl"), split_axis=1, concat_axis=2, tiled=True)
    expert_sum = jnp.sum(
        pieces.reshape(2, row_count, groups, full_width), axis=2, dtype=jnp.float32
    )
    grad_experts = outer_experts[0] - expert_sum / groups
    dense_sum, small_sum = (
        lax.psum_scatter(
            inner_dense[0].astype(jnp.float32).astype(jnp.bfloat16),
            "rep",
            scatter_dimension=1,
            tiled=True,
        ).astype(jnp.float32),
        lax.psum_scatter(
            inner_small[0].astype(jnp.float32).astype(jnp.bfloat16),
            "rep",
            scatter_dimension=1,
            tiled=True,
        ).astype(jnp.float32),
    )
    grad_dense = outer_dense - dense_sum / groups
    grad_small = outer_small - small_sum / groups
    col_count = outer_embed.shape[1]
    offset = lax.axis_index("rep") * col_count
    basis_part = lax.dynamic_slice_in_dim(embed_basis, offset, col_count, 0)
    partial_value = jnp.dot(
        outer_embed, basis_part, precision=lax.Precision.HIGHEST, preferred_element_type=jnp.float32
    )
    partial_value = (
        partial_value
        - jnp.dot(
            inner_embed[0].astype(jnp.float32),
            embed_basis,
            precision=lax.Precision.HIGHEST,
            preferred_element_type=jnp.float32,
        )
        / groups
    )
    coefficient = lax.psum(partial_value, "rep")
    grad_embed = jnp.dot(
        coefficient,
        basis_part.T,
        precision=lax.Precision.HIGHEST,
        preferred_element_type=jnp.float32,
    )
    expert_outer, expert_moment = nesterov(outer_experts[0], moment_experts[0], grad_experts)
    dense_outer, dense_moment = nesterov(outer_dense, moment_dense, grad_dense)
    small_outer, small_moment = nesterov(outer_small, moment_small, grad_small)
    embed_outer, embed_moment = nesterov(outer_embed, moment_embed, grad_embed)
    spread = lax.all_to_all(
        expert_outer.astype(jnp.bfloat16), "mdl", split_axis=2, concat_axis=1, tiled=True
    )
    copies = (
        lax.all_gather(spread, "rep", axis=1, tiled=True),
        lax.all_gather(dense_outer.astype(jnp.bfloat16), "rep", axis=1, tiled=True),
        lax.all_gather(small_outer.astype(jnp.bfloat16), "rep", axis=1, tiled=True),
        lax.all_gather(embed_outer.astype(jnp.bfloat16), "rep", axis=1, tiled=True),
    )
    return (
        expert_outer[None],
        expert_moment[None],
        copies[0][None],
        dense_outer,
        dense_moment,
        copies[1],
        small_outer,
        small_moment,
        copies[2],
        embed_outer,
        embed_moment,
        copies[3],
    )


def solution(mesh):
    placed = (
        P("rep", "exp", None, None, "mdl"),
        P("rep", ("exp", "mdl"), None),
        P("rep", None, None),
        P("rep", ("exp", "mdl"), None),
        P("exp", None, ("rep", "mdl"), None),
        P(("exp", "mdl"), "rep"),
        P(None, "rep"),
        P(("exp", "mdl"), "rep"),
        P("exp", None, ("rep", "mdl"), None),
        P(("exp", "mdl"), "rep"),
        P(None, "rep"),
        P(("exp", "mdl"), "rep"),
        P(),
    )
    return jax.shard_map(
        on_device,
        mesh=mesh,
        in_specs=placed,
        out_specs=(
            P("exp", None, ("rep", "mdl"), None),
            P("exp", None, ("rep", "mdl"), None),
            P("exp", None, None, "mdl"),
            P(("exp", "mdl"), "rep"),
            P(("exp", "mdl"), "rep"),
            P(("exp", "mdl"), None),
            P(None, "rep"),
            P(None, "rep"),
            P(),
            P(("exp", "mdl"), "rep"),
            P(("exp", "mdl"), "rep"),
            P(("exp", "mdl"), None),
        ),
        check_vma=False,
    )
```

profile of v0, /device:TPU:68, one launch (start us, length us, event | category | flops | bytes accessed | tf_op | source)
XLA Modules:
  0.0 202.1 jit_solution(756205942519219298)
XLA Ops:
  7.2 2.9 %copy.73 = bf16[1,1,2,768,256]{4,2,3,1,0:T(2,128)(2,1)} copy(bf16[1,1,2,768,256]{4,3,2,1,0:T(8,128)(2,1)} %param.13) | data formatting | bytes 1572864 | tf_op args[0]
  10.1 15.0 %all-to-all-start = ((bf16[2,768,256]{2,0,1:T(2,128)(2,1)}), bf16[2,768,256]{2,0,1:T(2,128)(2,1)S(1)}, u32[]{:S(2)}, u32[]{:S(2)}) async-start(bf16[2,768,256]{2,0,1:T(2,128)(2,1)} %bitcast.75), calls=%async_computation | async-start | bytes 1572864 | tf_op jit(solution)/shard_map/all_to_all | solution.py:35
  25.2 0.8 copy.68
  26.1 0.8 copy.66
  27.0 0.3 convolution_bitcast_fusion
  27.3 0.2 fusion
  27.5 58.3 %psum.7 = f32[64,64]{0,1:T(8,128)S(1)} all-reduce(f32[64,64]{0,1:T(8,128)S(1)} %fusion), channel_id=1, replica_groups=mesh['rep'=4,'exp'=16,'mdl'=8] {'rep'}, use_global_device_ids=true, to_apply=%region_3.0 | all-reduce | flops 4096 | bytes 32768 | tf_op jit(solution)/shard_map/psum | solution.py:72
  85.8 1.0 convert_bitcast_fusion.1
  86.7 19.4 %all-gather.2 = bf16[4,192,64]{1,2,0:T(8,128)(2,1)S(1)} all-gather(bf16[1,192,64]{1,2,0:T(8,128)(2,1)S(1)} %get-tuple-element.36), channel_id=1, replica_groups=mesh['rep'=4,'exp'=16,'mdl'=8] {'rep'}, dimensions={0}, use_global_device_ids=true | all-gather | bytes 122880 | tf_op jit(solution)/shard_map/all_gather | solution.py:90
  106.2 0.1 copy.64
  106.3 0.8 reshape.49
  107.0 0.9 copy.69
  107.9 0.6 convert_bitcast_fusion.2
  108.6 17.3 %all-gather.1 = bf16[4,192,18]{1,2,0:T(8,128)(2,1)S(1)} all-gather(bf16[1,192,18]{1,2,0:T(8,128)(2,1)S(1)} %get-tuple-element.39), channel_id=1, replica_groups=mesh['rep'=4,'exp'=16,'mdl'=8] {'rep'}, dimensions={0}, use_global_device_ids=true | all-gather | bytes 34560 | tf_op jit(solution)/shard_map/all_gather | solution.py:89
  125.9 0.7 reshape.47
  126.6 0.9 copy.67
  127.5 0.3 copy.72
  127.8 0.7 reshape.42
  128.5 1.0 reduce_sum.9
  129.5 0.1 copy-done.2
  129.6 0.1 fusion.5
  129.8 0.7 copy.59
  130.5 2.0 reshape.54
  132.5 7.1 %all-to-all-start.1 = ((bf16[8,2,6144]{2,1,0:T(2,128)(2,1)}), bf16[8,2,6144]{2,1,0:T(2,128)(2,1)S(1)}, u32[]{:S(2)}, u32[]{:S(2)}) async-start(bf16[8,2,6144]{2,1,0:T(2,128)(2,1)} %reshape.54), calls=%async_computation.1 | async-start | bytes 393216 | tf_op jit(solution)/shard_map/all_to_all | solution.py:83
  139.6 0.7 convert_bitcast_fusion
  140.3 17.7 %all-gather = bf16[4,192,72]{1,2,0:T(8,128)(2,1)S(1)} all-gather(bf16[1,192,72]{1,2,0:T(8,128)(2,1)S(1)} %get-tuple-element.42), channel_id=1, replica_groups=mesh['rep'=4,'exp'=16,'mdl'=8] {'rep'}, dimensions={0}, use_global_device_ids=true | all-gather | bytes 138240 | tf_op jit(solution)/shard_map/all_gather | solution.py:88
  158.1 0.8 reshape.45
  158.9 1.0 multiply_subtract_fusion
  159.9 1.5 reshape.55
  161.4 0.6 copy.60
  162.0 32.3 %all_gather.12 = bf16[2,768,256]{2,1,0:T(8,128)(2,1)S(1)} all-gather(bf16[2,192,256]{2,1,0:T(8,128)(2,1)S(1)} %bitcast.83), channel_id=1, replica_groups=mesh['rep'=4,'exp'=16,'mdl'=8] {'rep'}, dimensions={1}, use_global_device_ids=true | all-gather | bytes 983040 | tf_op jit(solution)/shard_map/all_gather | solution.py:87
  194.4 0.9 copy.75
  (33 shorter events, 0.3 us)
Async XLA Ops:
  7.2 19.8 %copy-start = (f32[768,64]{0,1:T(8,128)S(1)}, f32[768,64]{0,1:T(8,128)}, u32[]{:S(2)}) copy-start(f32[768,64]{0,1:T(8,128)} %param.25) | copy-start | bytes 589828
  7.2 18.0 %copy-start.9 = (bf16[1,18,768]{2,1,0:T(8,128)(2,1)S(1)}, bf16[1,18,768]{2,1,0:T(8,128)(2,1)}, u32[]{:S(2)}) copy-start(bf16[1,18,768]{2,1,0:T(8,128)(2,1)} %param.15) | copy-start | bytes 82948
  7.2 18.9 %copy-start.4 = (bf16[1,72,768]{2,1,0:T(8,128)(2,1)S(1)}, bf16[1,72,768]{2,1,0:T(8,128)(2,1)}, u32[]{:S(2)}) copy-start(bf16[1,72,768]{2,1,0:T(8,128)(2,1)} %param.14) | copy-start | bytes 331780
  10.1 16.9 %copy-start.3 = (f32[64,192]{1,0:T(8,128)S(1)}, f32[64,192]{1,0:T(8,128)}, u32[]{:S(2)}) copy-start(f32[64,192]{1,0:T(8,128)} %param.20) | copy-start | bytes 147460
  10.1 17.2 %copy-start.5 = (bf16[1,64,768]{2,1,0:T(8,128)(2,1)S(1)}, bf16[1,64,768]{2,1,0:T(8,128)(2,1)}, u32[]{:S(2)}) copy-start(bf16[1,64,768]{2,1,0:T(8,128)(2,1)} %param.16) | copy-start | bytes 294916
  10.1 75.7 %copy-start.8 = (f32[64,192]{1,0:T(8,128)S(1)}, f32[64,192]{1,0:T(8,128)}, u32[]{:S(2)}) copy-start(f32[64,192]{1,0:T(8,128)} %param.24) | copy-start | bytes 147460
  10.1 117.4 %all-to-all-start = ((bf16[2,768,256]{2,0,1:T(2,128)(2,1)}), bf16[2,768,256]{2,0,1:T(2,128)(2,1)S(1)}, u32[]{:S(2)}, u32[]{:S(2)}) async-start(bf16[2,768,256]{2,0,1:T(2,128)(2,1)} %bitcast.75), calls=%async_computation | async-start | bytes 1572864 | tf_op jit(solution)/shard_map/all_to_all | solution.py:35
  25.1 82.8 %copy-start.10 = (f32[18,192]{1,0:T(8,128)S(1)}, f32[18,192]{1,0:T(8,128)}, u32[]{:S(2)}) copy-start(f32[18,192]{1,0:T(8,128)} %param.19) | copy-start | bytes 41476
  25.1 82.8 %copy-start.11 = (f32[18,192]{1,0:T(8,128)S(1)}, f32[18,192]{1,0:T(8,128)}, u32[]{:S(2)}) copy-start(f32[18,192]{1,0:T(8,128)} %param.23) | copy-start | bytes 41476
  25.2 81.9 %reduce-scatter.9.cloned.1.call-start = ((), (), s32[]{:S(2)}) async-start(), calls=%async_computation.5 | async-start | bytes 245760
  26.1 100.5 %reduce-scatter.7.cloned.1.call-start = ((), (), s32[]{:S(2)}) async-start(), calls=%async_computation.4 | async-start | bytes 245760
  128.5 1.0 copy-start.1
  128.5 1.1 copy-start.2
  129.8 9.9 %copy-start.6 = (f32[72,192]{1,0:T(8,128)S(1)}, f32[72,192]{1,0:T(8,128)}, u32[]{:S(2)}) copy-start(f32[72,192]{1,0:T(8,128)} %param.18) | copy-start | bytes 165892
  129.8 9.9 %copy-start.7 = (f32[72,192]{1,0:T(8,128)S(1)}, f32[72,192]{1,0:T(8,128)}, u32[]{:S(2)}) copy-start(f32[72,192]{1,0:T(8,128)} %param.22) | copy-start | bytes 165892
  132.5 27.4 %all-to-all-start.1 = ((bf16[8,2,6144]{2,1,0:T(2,128)(2,1)}), bf16[8,2,6144]{2,1,0:T(2,128)(2,1)S(1)}, u32[]{:S(2)}, u32[]{:S(2)}) async-start(bf16[8,2,6144]{2,1,0:T(2,128)(2,1)} %reshape.54), calls=%async_computation.1 | async-start | bytes 393216 | tf_op jit(solution)/shard_map/all_to_all | solution.py:83
Sparse Core Ops, SparseCore 0:
  29.3 40.5 reduce-scatter.8
  73.3 35.0 reduce-scatter.6
where the time goes:
time: 203 us; the launch traced here: 202 us
  blocking collectives  145 us (71%)
  starting transfers between devices  22.2 us (11%)
  local copies, waits for them, and re-layouts  15.6 us (8%)
  between operations  14.3 us (7%)
  other arithmetic  3.39 us (2%)
    psum x1, blocking collectives, on_device(): coefficient = lax.psum(partial_value, 'rep')  58.3 us
    all_gather x1, blocking collectives, on_device(): lax.all_gather(spread, 'rep', axis=1, tiled=True)  32.3 us
    all_gather x1, blocking collectives, on_device(): lax.all_gather(embed_outer.astype(jnp.bfloat16), 'rep', axis=1, tiled=True)  19.4 us
    all_gather x1, blocking collectives, on_device(): lax.all_gather(dense_outer.astype(jnp.bfloat16), 'rep', axis=1, tiled=True)  17.7 us
    all_gather x1, blocking collectives, on_device(): lax.all_gather(small_outer.astype(jnp.bfloat16), 'rep', axis=1, tiled=True)  17.3 us
    all_to_all x1, starting transfers between devices, on_device(): lax.all_to_all(own_shard, ('rep', 'mdl'), split_axis=1, concat_axis=2, ti...  15 us
    unnamed x35, local copies, waits for them, and re-layouts  13.1 us
    all_to_all x1, starting transfers between devices, on_device(): lax.all_to_all(expert_outer.astype(jnp.bfloat16), 'mdl', split_axis=2, co...  7.09 us
  transfers between devices with their start and end apart: 4, of which 0 were waited for; matrix products, arithmetic and copies ran while one was open for 5% of the time, Pallas kernels for 0%

commit v1 on v0

--- a/solution.py
+++ b/solution.py
@@ -87,7 +87,12 @@
         lax.all_gather(spread, "rep", axis=1, tiled=True),
         lax.all_gather(dense_outer.astype(jnp.bfloat16), "rep", axis=1, tiled=True),
         lax.all_gather(small_outer.astype(jnp.bfloat16), "rep", axis=1, tiled=True),
-        lax.all_gather(embed_outer.astype(jnp.bfloat16), "rep", axis=1, tiled=True),
+        jnp.concatenate(
+            lax.all_to_all(
+                jnp.stack([embed_outer.astype(jnp.bfloat16)] * lax.axis_size("rep")), "rep", 0, 0
+            ),
+            axis=1,
+        ),
     )
     return (
         expert_outer[None],

time: 203 us -> 200 us (0.985)
  the two profiles are of different devices: /device:TPU:68 before, /device:TPU:92 now
where the time goes in v1:
time: 200 us
  blocking collectives  128 us (64%)
  starting transfers between devices  28.2 us (14%)
  local copies, waits for them, and re-layouts  16.3 us (8%)
  between operations  14.3 us (7%)
  waiting for transfers between devices  8.2 us (4%)
  other arithmetic  3.39 us (2%)
    psum x1, blocking collectives, on_device(): coefficient = lax.psum(partial_value, 'rep')  59.2 us
    all_gather x1, blocking collectives, on_device(): lax.all_gather(spread, 'rep', axis=1, tiled=True)  32.9 us
    all_gather x1, blocking collectives, on_device(): lax.all_gather(dense_outer.astype(jnp.bfloat16), 'rep', axis=1, tiled=True)  17.8 us
    all_gather x1, blocking collectives, on_device(): lax.all_gather(small_outer.astype(jnp.bfloat16), 'rep', axis=1, tiled=True)  17.8 us
    all_to_all x1, starting transfers between devices, on_device(): lax.all_to_all(own_shard, ('rep', 'mdl'), split_axis=1, concat_axis=2, ti...  15 us
    unnamed x34, local copies, waits for them, and re-layouts  12.3 us
    all_to_all x1, waiting for transfers between devices, on_device(): lax.all_to_all(jnp.stack([embed_outer.astype(jnp.bfloat16)] * lax.axis_si...  8.16 us
    all_to_all x1, starting transfers between devices, on_device(): lax.all_to_all(jnp.stack([embed_outer.astype(jnp.bfloat16)] * lax.axis_si...  6.58 us
  transfers between devices with their start and end apart: 5, of which 1 were waited for; matrix products, arithmetic and copies ran while one was open for 7% of the time, Pallas kernels for 0%

profile of v1, /device:TPU:92, one launch (start us, length us, event | category | flops | bytes accessed | tf_op | source)
XLA Modules:
  0.0 199.6 jit_solution(8712636283003313583)
XLA Ops:
  7.2 2.9 %copy.71 = bf16[1,1,2,768,256]{4,2,3,1,0:T(2,128)(2,1)} copy(bf16[1,1,2,768,256]{4,3,2,1,0:T(8,128)(2,1)} %param.13) | data formatting | bytes 1572864 | tf_op args[0]
  10.1 15.0 %all-to-all-start = ((bf16[2,768,256]{2,0,1:T(2,128)(2,1)}), bf16[2,768,256]{2,0,1:T(2,128)(2,1)S(1)}, u32[]{:S(2)}, u32[]{:S(2)}) async-start(bf16[2,768,256]{2,0,1:T(2,128)(2,1)} %bitcast.69), calls=%async_computation | async-start | bytes 1572864 | tf_op jit(solution)/shard_map/all_to_all | solution.py:35
  25.2 0.8 copy.66
  26.1 0.8 copy.64
  27.0 0.3 convolution_bitcast_fusion
  27.3 0.2 fusion
  27.5 59.2 %psum.7 = f32[64,64]{0,1:T(8,128)S(1)} all-reduce(f32[64,64]{0,1:T(8,128)S(1)} %fusion), channel_id=1, replica_groups=mesh['rep'=4,'exp'=16,'mdl'=8] {'rep'}, use_global_device_ids=true, to_apply=%region_3.0 | all-reduce | flops 4096 | bytes 32768 | tf_op jit(solution)/shard_map/psum | solution.py:72
  86.7 1.0 fusion.12
  87.7 0.9 copy.67
  88.5 0.6 convert_bitcast_fusion.1
  89.2 17.8 %all-gather.1 = bf16[4,192,18]{1,2,0:T(8,128)(2,1)S(1)} all-gather(bf16[1,192,18]{1,2,0:T(8,128)(2,1)S(1)} %get-tuple-element.39), channel_id=1, replica_groups=mesh['rep'=4,'exp'=16,'mdl'=8] {'rep'}, dimensions={0}, use_global_device_ids=true | all-gather | bytes 34560 | tf_op jit(solution)/shard_map/all_gather | solution.py:89
  107.0 0.7 reshape.57
  107.7 0.9 copy.65
  108.6 0.7 stack.2
  109.3 6.6 %all-to-all-start.2 = ((bf16[4,64,192]{2,1,0:T(8,128)(2,1)}), bf16[4,64,192]{2,1,0:T(8,128)(2,1)S(1)}, u32[]{:S(2)}, u32[]{:S(2)}) async-start(bf16[4,64,192]{2,1,0:T(8,128)(2,1)} %stack.2), calls=%async_computation.2 | async-start | bytes 262144 | tf_op jit(solution)/shard_map/all_to_all | solution.py:91
  115.9 0.3 copy.70
  116.1 0.7 reshape.52
  116.9 1.0 reduce_sum.9
  118.0 0.1 fusion.5
  118.2 0.7 copy.57
  118.9 2.0 %reshape.62 = bf16[8,2,6144]{2,1,0:T(2,128)(2,1)} reshape(bf16[2048,2,24]{2,1,0:T(2,128)(2,1)S(1)} %bitcast.71) | data formatting | bytes 393216
  120.9 8.2 %all-to-all-done.2 = bf16[4,64,192]{2,1,0:T(8,128)(2,1)S(1)} async-done(((bf16[4,64,192]{2,1,0:T(8,128)(2,1)}), bf16[4,64,192]{2,1,0:T(8,128)(2,1)S(1)}, u32[]{:S(2)}, u32[]{:S(2)}) %all-to-all-start.2) | async-done | bytes 98336 | tf_op jit(solution)/shard_map/all_to_all | solution.py:91
  129.1 6.5 %all-to-all-start.1 = ((bf16[8,2,6144]{2,1,0:T(2,128)(2,1)}), bf16[8,2,6144]{2,1,0:T(2,128)(2,1)S(1)}, u32[]{:S(2)}, u32[]{:S(2)}) async-start(bf16[8,2,6144]{2,1,0:T(2,128)(2,1)} %reshape.62), calls=%async_computation.1 | async-start | bytes 393216 | tf_op jit(solution)/shard_map/all_to_all | solution.py:83
  135.6 0.7 convert_bitcast_fusion
  136.3 17.8 %all-gather = bf16[4,192,72]{1,2,0:T(8,128)(2,1)S(1)} all-gather(bf16[1,192,72]{1,2,0:T(8,128)(2,1)S(1)} %get-tuple-element.42), channel_id=1, replica_groups=mesh['rep'=4,'exp'=16,'mdl'=8] {'rep'}, dimensions={0}, use_global_device_ids=true | all-gather | bytes 138240 | tf_op jit(solution)/shard_map/all_gather | solution.py:88
  154.2 0.8 reshape.55
  155.1 0.8 reshape.51
  155.8 1.0 multiply_subtract_fusion
  156.8 1.5 reshape.63
  158.3 0.6 copy.58
  158.9 32.9 %all_gather.9 = bf16[2,768,256]{2,1,0:T(8,128)(2,1)S(1)} all-gather(bf16[2,192,256]{2,1,0:T(8,128)(2,1)S(1)} %bitcast.77), channel_id=1, replica_groups=mesh['rep'=4,'exp'=16,'mdl'=8] {'rep'}, dimensions={1}, use_global_device_ids=true | all-gather | bytes 983040 | tf_op jit(solution)/shard_map/all_gather | solution.py:87
  191.9 0.9 copy.73
  (35 shorter events, 0.5 us)
Async XLA Ops:
  7.2 19.8 %copy-start = (f32[768,64]{0,1:T(8,128)S(1)}, f32[768,64]{0,1:T(8,128)}, u32[]{:S(2)}) copy-start(f32[768,64]{0,1:T(8,128)} %param.25) | copy-start | bytes 589828
  7.2 18.0 %copy-start.9 = (bf16[1,18,768]{2,1,0:T(8,128)(2,1)S(1)}, bf16[1,18,768]{2,1,0:T(8,128)(2,1)}, u32[]{:S(2)}) copy-start(bf16[1,18,768]{2,1,0:T(8,128)(2,1)} %param.15) | copy-start | bytes 82948
  7.2 18.9 %copy-start.4 = (bf16[1,72,768]{2,1,0:T(8,128)(2,1)S(1)}, bf16[1,72,768]{2,1,0:T(8,128)(2,1)}, u32[]{:S(2)}) copy-start(bf16[1,72,768]{2,1,0:T(8,128)(2,1)} %param.14) | copy-start | bytes 331780
  10.1 16.9 %copy-start.3 = (f32[64,192]{1,0:T(8,128)S(1)}, f32[64,192]{1,0:T(8,128)}, u32[]{:S(2)}) copy-start(f32[64,192]{1,0:T(8,128)} %param.20) | copy-start | bytes 147460
  10.1 17.2 %copy-start.5 = (bf16[1,64,768]{2,1,0:T(8,128)(2,1)S(1)}, bf16[1,64,768]{2,1,0:T(8,128)(2,1)}, u32[]{:S(2)}) copy-start(bf16[1,64,768]{2,1,0:T(8,128)(2,1)} %param.16) | copy-start | bytes 294916
  10.1 76.6 %copy-start.8 = (f32[64,192]{1,0:T(8,128)S(1)}, f32[64,192]{1,0:T(8,128)}, u32[]{:S(2)}) copy-start(f32[64,192]{1,0:T(8,128)} %param.24) | copy-start | bytes 147460
  10.1 78.4 %copy-start.10 = (f32[18,192]{1,0:T(8,128)S(1)}, f32[18,192]{1,0:T(8,128)}, u32[]{:S(2)}) copy-start(f32[18,192]{1,0:T(8,128)} %param.19) | copy-start | bytes 41476
  10.1 78.4 %copy-start.11 = (f32[18,192]{1,0:T(8,128)S(1)}, f32[18,192]{1,0:T(8,128)}, u32[]{:S(2)}) copy-start(f32[18,192]{1,0:T(8,128)} %param.23) | copy-start | bytes 41476
  10.1 98.5 %all-to-all-start = ((bf16[2,768,256]{2,0,1:T(2,128)(2,1)}), bf16[2,768,256]{2,0,1:T(2,128)(2,1)S(1)}, u32[]{:S(2)}, u32[]{:S(2)}) async-start(bf16[2,768,256]{2,0,1:T(2,128)(2,1)} %bitcast.69), calls=%async_computation | async-start | bytes 1572864 | tf_op jit(solution)/shard_map/all_to_all | solution.py:35
  25.2 62.5 %reduce-scatter.9.cloned.1.call-start = ((), (), s32[]{:S(2)}) async-start(), calls=%async_computation.6 | async-start | bytes 245760
  26.1 81.7 %reduce-scatter.7.cloned.1.call-start = ((), (), s32[]{:S(2)}) async-start(), calls=%async_computation.5 | async-start | bytes 245760
  109.3 19.8 %all-to-all-start.2 = ((bf16[4,64,192]{2,1,0:T(8,128)(2,1)}), bf16[4,64,192]{2,1,0:T(8,128)(2,1)S(1)}, u32[]{:S(2)}, u32[]{:S(2)}) async-start(bf16[4,64,192]{2,1,0:T(8,128)(2,1)} %stack.2), calls=%async_computation.2 | async-start | bytes 262144 | tf_op jit(solution)/shard_map/all_to_all | solution.py:91
  116.9 1.0 copy-start.1
  116.9 1.1 copy-start.2
  118.1 17.4 %copy-start.6 = (f32[72,192]{1,0:T(8,128)S(1)}, f32[72,192]{1,0:T(8,128)}, u32[]{:S(2)}) copy-start(f32[72,192]{1,0:T(8,128)} %param.18) | copy-start | bytes 165892
  118.1 17.4 %copy-start.7 = (f32[72,192]{1,0:T(8,128)S(1)}, f32[72,192]{1,0:T(8,128)}, u32[]{:S(2)}) copy-start(f32[72,192]{1,0:T(8,128)} %param.22) | copy-start | bytes 165892
  129.1 27.8 %all-to-all-start.1 = ((bf16[8,2,6144]{2,1,0:T(2,128)(2,1)}), bf16[8,2,6144]{2,1,0:T(2,128)(2,1)S(1)}, u32[]{:S(2)}, u32[]{:S(2)}) async-start(bf16[8,2,6144]{2,1,0:T(2,128)(2,1)} %reshape.62), calls=%async_computation.1 | async-start | bytes 393216 | tf_op jit(solution)/shard_map/all_to_all | solution.py:83
Sparse Core Ops, SparseCore 0:
  29.3 40.9 reduce-scatter.8
  73.7 33.4 reduce-scatter.6
